TPU v7x, 256 devices: a whole 4x4x8 slice. The times are simulated.
256 devices in a mesh: dp: 64 (over x, z, core), tensor: 4 (over y).
Axes of the slice: x: 4, y: 4, z: 8, core: 2. Of those that a mesh axis runs over, the one named last changes fastest.
Arguments:
- attention_grads: bfloat16 [64, 1, 512, 2048], P('dp', None, None, 'tensor')
- expert_grads: bfloat16 [64, 1, 2, 512, 4096], P('dp', None, None, None, 'tensor')
- routing_grads: bfloat16 [64, 4, 1, 36, 512], P('dp', 'tensor'), may hold values from -640 to 640
- attention_master: float32 [512, 2048], P('dp', 'tensor'), may hold values from -0.25 to 0.25
- attention_first: float32 [512, 2048], P('dp', 'tensor'), may hold values from -4 to 4
- attention_second: float32 [512, 2048], P('dp', 'tensor'), may hold values from 0.05 to 2
- expert_master: float32 [2, 512, 4096], P(None, 'dp', 'tensor'), may hold values from -0.25 to 0.25
- expert_first: float32 [2, 512, 4096], P(None, 'dp', 'tensor'), may hold values from -4 to 4
- expert_second: float32 [2, 512, 4096], P(None, 'dp', 'tensor'), may hold values from 0.05 to 2
- routing_master: float32 [36, 512], P(None, ('dp', 'tensor')), may hold values from -4 to 4
- routing_first: float32 [36, 512], P(None, ('dp', 'tensor')), may hold values from -4 to 4
- routing_second: float32 [36, 512], P(None, ('dp', 'tensor')), may hold values from 0.05 to 2
- step_count: int32 [1], replicated, may hold values from 1 to 1000
- learn_rate: float32 [1], replicated, may hold values from 0.05 to 0.3
- clip_level: float32 [1], replicated, may hold values from 0.5 to 2
Outputs:
- attention_renewed: float32 [512, 2048], P('dp', 'tensor')
- attention_momentum: float32 [512, 2048], P('dp', 'tensor')
- attention_variance: float32 [512, 2048], P('dp', 'tensor')
- attention_served: bfloat16 [512, 2048], P(None, 'tensor')
- expert_renewed: float32 [2, 512, 4096], P(None, 'dp', 'tensor')
- expert_momentum: float32 [2, 512, 4096], P(None, 'dp', 'tensor')
- expert_variance: float32 [2, 512, 4096], P(None, 'dp', 'tensor')
- expert_served: bfloat16 [2, 512, 4096], P(None, None, 'tensor')
- routing_renewed: float32 [36, 512], P(None, ('dp', 'tensor'))
- routing_momentum: float32 [36, 512], P(None, ('dp', 'tensor'))
- routing_variance: float32 [36, 512], P(None, ('dp', 'tensor'))
- routing_served: bfloat16 [36, 512], replicated
Inputs may be any that keep to these rules, and one draw needn't show every extreme that they name: `step_count`: the number of optimizer steps taken, this one included.
All inputs are finite; a program needn't handle non-finite values.
Results may differ from a plain program's by a relative error of at most 0.0004.
Values may be sent and summed in bfloat16 or wider, within the bound.
No kernel may reach another device: no remote copies, remote signals or barrier semaphores. Data moves between devices by JAX's collectives and lax.ppermute only.
A program may use at most 64 MiB of HBM per device.

v0:
```python
from functools import reduce
import jax
import jax.numpy as jnp
from jax import lax
from jax.sharding import PartitionSpec as P

EXPERTS = 32
PARAMS = 5261312
BETA_ONE = 0.9
BETA_TWO = 0.999
EPSILON = 1e-08
DECAY = 0.1


def micro_total(blocks):
    return reduce(lambda left, right: left + right, [blocks[0].astype(jnp.float32)])


def adam_update(grad_sum, master, first, second, clip, rate, first_fix, second_fix, mask):
    grad = clip * grad_sum
    momentum = BETA_ONE * first + (1.0 - BETA_ONE) * grad
    variance = BETA_TWO * second + (1.0 - BETA_TWO) * grad * grad
    update = (
        momentum / first_fix / (jnp.sqrt(variance / second_fix) + EPSILON) + DECAY * mask * master
    )
    renewed = master - rate * update
    return (renewed, momentum, variance, renewed.astype(jnp.bfloat16))


def local(
    attention_grads,
    expert_grads,
    routing_grads,
    attention_master,
    attention_first,
    attention_second,
    expert_master,
    expert_first,
    expert_second,
    routing_master,
    routing_first,
    routing_second,
    step_count,
    learn_rate,
    clip_level,
):
    attention_local = attention_grads[0]
    expert_local = expert_grads[0]
    attention_sum = lax.psum_scatter(
        micro_total(attention_local), "dp", scatter_dimension=0, tiled=True
    )
    expert_sum = lax.psum_scatter(micro_total(expert_local), "dp", scatter_dimension=1, tiled=True)
    expert_pieces = [expert_sum[index] for index in range(expert_sum.shape[0])]
    routing_local = micro_total(routing_grads[0, 0])
    routing_sum = lax.psum_scatter(routing_local, ("dp", "tensor"), scatter_dimension=1, tiled=True)
    expert_squares = reduce(
        lambda left, right: left + right, [jnp.sum(piece * piece) for piece in expert_pieces]
    )
    attention_total, expert_total, routing_total = lax.psum(
        (
            jnp.sum(attention_sum * attention_sum),
            expert_squares,
            jnp.sum(routing_sum * routing_sum),
        ),
        ("dp", "tensor"),
    )
    grad_norm = jnp.sqrt(attention_total + expert_total + routing_total)
    clip = jnp.minimum(1.0, clip_level[0] * jnp.sqrt(jnp.float32(PARAMS)) / (grad_norm + 1e-06))
    steps_done = step_count[0].astype(jnp.float32)
    first_fix = 1.0 - jnp.power(jnp.float32(BETA_ONE), steps_done)
    second_fix = 1.0 - jnp.power(jnp.float32(BETA_TWO), steps_done)
    rate = learn_rate[0]
    attention_out = adam_update(
        attention_sum,
        attention_master,
        attention_first,
        attention_second,
        clip,
        rate,
        first_fix,
        second_fix,
        jnp.float32(1.0),
    )
    attention_served = lax.all_gather(attention_out[3], "dp", axis=0, tiled=True)
    expert_sum = jnp.stack(expert_pieces, axis=0)
    expert_out = adam_update(
        expert_sum,
        expert_master,
        expert_first,
        expert_second,
        clip,
        rate,
        first_fix,
        second_fix,
        jnp.float32(1.0),
    )
    expert_renewed, expert_momentum, expert_variance = (expert_out[0], expert_out[1], expert_out[2])
    expert_served = lax.all_gather(expert_out[3], "dp", axis=1, tiled=True)
    row_index = jnp.arange(routing_master.shape[0], dtype=jnp.int32)
    routing_mask = (row_index < EXPERTS).astype(jnp.float32)[:, None]
    routing_out = adam_update(
        routing_sum,
        routing_master,
        routing_first,
        routing_second,
        clip,
        rate,
        first_fix,
        second_fix,
        routing_mask,
    )
    routing_served = lax.all_gather(routing_out[3], ("dp", "tensor"), axis=1, tiled=True)
    return (
        attention_out[0],
        attention_out[1],
        attention_out[2],
        attention_served,
        expert_renewed,
        expert_momentum,
        expert_variance,
        expert_served,
        routing_out[0],
        routing_out[1],
        routing_out[2],
        routing_served,
    )


def solution(mesh):
    in_specs = (
        P("dp", None, None, "tensor"),
        P("dp", None, None, None, "tensor"),
        P("dp", "tensor", None, None, None),
        P("dp", "tensor"),
        P("dp", "tensor"),
        P("dp", "tensor"),
        P(None, "dp", "tensor"),
        P(None, "dp", "tensor"),
        P(None, "dp", "tensor"),
        P(None, ("dp", "tensor")),
        P(None, ("dp", "tensor")),
        P(None, ("dp", "tensor")),
        P(),
        P(),
        P(),
    )
    out_specs = (
        P("dp", "tensor"),
        P("dp", "tensor"),
        P("dp", "tensor"),
        P(None, "tensor"),
        P(None, "dp", "tensor"),
        P(None, "dp", "tensor"),
        P(None, "dp", "tensor"),
        P(None, None, "tensor"),
        P(None, ("dp", "tensor")),
        P(None, ("dp", "tensor")),
        P(None, ("dp", "tensor")),
        P(),
    )
    return jax.shard_map(local, mesh=mesh, in_specs=in_specs, out_specs=out_specs, check_vma=False)
```

profile of v0, /device:TPU:1, one launch (start us, length us, event | category | flops | bytes accessed | tf_op | source)
XLA Modules:
  0.0 543.5 jit_solution(8500737560989414469)
XLA Ops:
  8.0 0.0 copy-start
  8.0 0.0 all-reduce.3.cloned.1.call-start
  8.1 1.1 copy.29
  9.1 0.7 bitcast_convert_fusion.2
  9.9 0.0 all-reduce.3.cloned.1.call-update
  9.9 0.0 reduce-scatter.3.cloned.1.call-start
  9.9 2.1 bitcast_convert_fusion.1
  12.1 0.0 reduce-scatter.3.cloned.1.call-update
  12.1 0.0 reduce-scatter.5.cloned.1.call-start
  12.2 0.0 copy-done
  12.2 2.4 bitcast_convert_fusion
  14.6 0.0 copy-start.1
  14.6 0.0 copy-start.2
  14.6 0.0 copy-start.3
  14.6 0.0 copy-start.7
  14.6 0.0 copy-start.8
  14.6 0.0 copy-start.9
  14.6 0.0 copy-start.4
  14.6 0.0 copy-start.5
  14.6 0.0 copy-start.6
  14.6 0.0 reduce-scatter.5.cloned.1.call-update
  14.7 0.0 all-gather.3.cloned.1.call-start
  16.8 256.6 %all-reduce.3.cloned.1.call-done = f32[36,512]{0,1:T(8,128)} async-done(((f32[36,512]{0,1:T(8,128)}), f32[36,512]{0,1:T(8,128)}) %all-reduce.3.cloned.1.call-update) | async-done | bytes 73744
  273.4 1.3 multiply_reduce_fusion.1
  274.7 0.0 reduce-scatter.3.cloned.1.call-done
  274.7 1.3 multiply_reduce_fusion
  276.0 24.4 %reduce-scatter.5.cloned.1.call-done = f32[2,8,1024]{2,1,0:T(8,128)} async-done(((f32[2,512,1024]{2,1,0:T(8,128)}), f32[2,8,1024]{2,1,0:T(8,128)}) %reduce-scatter.5.cloned.1.call-update) | async-done | bytes 65552 | tf_op jit(solution)/shard_map/reduce_scatter | solution.py:52
  300.5 1.4 fusion.1
  304.5 79.6 %psum.25 = f32[]{:T(128)} all-reduce(f32[]{:T(128)S(6)} %add.71), channel_id=1, replica_groups=mesh['dp'=64,'tensor'=4] {'dp','tensor'}, use_global_device_ids=true, to_apply=%region_2.0 | all-reduce | flops 1 | bytes 8 | tf_op jit(solution)/shard_map/psum | solution.py:59
  384.8 0.0 copy-done.1
  384.8 0.0 copy-done.2
  384.9 0.0 copy-done.3
  384.9 1.5 fusion.6
  386.4 0.0 all-gather.3.cloned.1.call-update
  386.4 0.0 copy-done.7
  386.5 0.0 copy-done.8
  386.5 0.0 copy-done.9
  386.5 1.3 convert_bitcast_fusion
  387.8 93.8 %all-gather = bf16[256,2,36]{2,1,0:T(2,128)(2,1)S(1)} all-gather(bf16[1,2,36]{2,1,0:T(2,128)(2,1)S(1)} %get-tuple-element.14), channel_id=1, replica_groups=mesh['dp'=64,'tensor'=4] {'dp','tensor'}, dimensions={0}, use_global_device_ids=true | all-gather | bytes 37008 | tf_op jit(solution)/shard_map/all_gather | solution.py:112
  481.5 0.7 copy.30
  482.3 0.0 copy-done.4
  482.3 0.0 copy-done.5
  482.3 0.0 copy-done.6
  482.3 1.4 fusion.8
  483.6 48.4 %all_gather.9 = bf16[512,512]{1,0:T(8,128)(2,1)S(1)} all-gather(bf16[8,512]{1,0:T(8,128)(2,1)S(1)} %get-tuple-element.22), channel_id=1, replica_groups=mesh['dp'=64,'tensor'=4] {'dp'}, dimensions={0}, use_global_device_ids=true | all-gather | bytes 532480 | tf_op jit(solution)/shard_map/all_gather | solution.py:84
  532.1 0.0 all-gather.3.cloned.1.call-done
  532.1 0.8 copy.37
  532.9 3.1 copy.38
  (1 shorter events, 0.0 us)
Async XLA Ops:
  8.0 4.1 copy-start
  8.0 265.4 %all-reduce.3.cloned.1.call-start = ((), (), s32[]{:S(2)}) async-start(), calls=%async_computation.5 | async-start | bytes 524288
  9.9 264.8 %reduce-scatter.3.cloned.1.call-start = ((), (), s32[]{:S(2)}) async-start(), calls=%async_computation.2 | async-start | bytes 1064960 | tf_op jit(solution)/shard_map/reduce_scatter | solution.py:49
  12.1 288.4 %reduce-scatter.5.cloned.1.call-start = ((), (), s32[]{:S(2)}) async-start(), calls=%async_computation.3 | async-start | bytes 4259840 | tf_op jit(solution)/shard_map/reduce_scatter | solution.py:52
  14.6 370.3 %copy-start.1 = (f32[2,8,1024]{2,1,0:T(8,128)S(1)}, f32[2,8,1024]{2,1,0:T(8,128)}, u32[]{:S(2)}) copy-start(f32[2,8,1024]{2,1,0:T(8,128)} %param.21) | copy-start | bytes 196612
  14.6 370.3 %copy-start.2 = (f32[2,8,1024]{2,1,0:T(8,128)S(1)}, f32[2,8,1024]{2,1,0:T(8,128)}, u32[]{:S(2)}) copy-start(f32[2,8,1024]{2,1,0:T(8,128)} %param.23) | copy-start | bytes 196612
  14.6 370.3 %copy-start.3 = (f32[2,8,1024]{2,1,0:T(8,128)S(1)}, f32[2,8,1024]{2,1,0:T(8,128)}, u32[]{:S(2)}) copy-start(f32[2,8,1024]{2,1,0:T(8,128)} %param.22) | copy-start | bytes 196612
  14.6 371.9 %copy-start.7 = (f32[36,2]{0,1:T(2,128)S(1)}, f32[36,2]{0,1:T(2,128)}, u32[]{:S(2)}) copy-start(f32[36,2]{0,1:T(2,128)} %param.24) | copy-start | bytes 868
  14.6 371.9 %copy-start.8 = (f32[36,2]{0,1:T(2,128)S(1)}, f32[36,2]{0,1:T(2,128)}, u32[]{:S(2)}) copy-start(f32[36,2]{0,1:T(2,128)} %param.26) | copy-start | bytes 868
  14.6 371.9 %copy-start.9 = (f32[36,2]{0,1:T(2,128)S(1)}, f32[36,2]{0,1:T(2,128)}, u32[]{:S(2)}) copy-start(f32[36,2]{0,1:T(2,128)} %param.25) | copy-start | bytes 868
  14.6 467.7 %copy-start.4 = (f32[8,512]{1,0:T(8,128)S(1)}, f32[8,512]{1,0:T(8,128)}, u32[]{:S(2)}) copy-start(f32[8,512]{1,0:T(8,128)} %param.18) | copy-start | bytes 49156
  14.6 467.7 %copy-start.5 = (f32[8,512]{1,0:T(8,128)S(1)}, f32[8,512]{1,0:T(8,128)}, u32[]{:S(2)}) copy-start(f32[8,512]{1,0:T(8,128)} %param.20) | copy-start | bytes 49156
  14.6 467.7 %copy-start.6 = (f32[8,512]{1,0:T(8,128)S(1)}, f32[8,512]{1,0:T(8,128)}, u32[]{:S(2)}) copy-start(f32[8,512]{1,0:T(8,128)} %param.19) | copy-start | bytes 49156
  14.7 517.4 %all-gather.3.cloned.1.call-start = ((), (), s32[]{:S(2)}) async-start(), calls=%async_computation.4 | async-start | bytes 2129920 | tf_op jit(solution)/shard_map/all_gather | solution.py:98
Sparse Core Ops, SparseCore 0:
  14.9 258.5 all-reduce.2
Sparse Core Ops, SparseCore 1:
  14.9 139.2 reduce-scatter.2
  158.2 142.3 reduce-scatter.4
  386.5 74.5 all-gather.2
where the time goes:
time: 544 us
  waiting for transfers between devices  281 us (52%)
  blocking collectives  222 us (41%)
  between operations  21.2 us (4%)
  other arithmetic  13.5 us (2%)
  local copies, waits for them, and re-layouts  5.73 us (1%)
    unnamed x5, waiting for transfers between devices  257 us
    all_gather x1, blocking collectives, local(): lax.all_gather(routing_out[3], ('dp', 'tensor'), axis=1, tiled=True)  93.8 us
    psum x1, blocking collectives, local(): lax.psum((jnp.sum(attention_sum * attention_sum), expert_squares, jnp.sum...  79.6 us
    all_gather x1, blocking collectives, local(): lax.all_gather(attention_out[3], 'dp', axis=0, tiled=True)  48.4 us
    reduce_scatter x1, waiting for transfers between devices, local(): lax.psum_scatter(micro_total(expert_local), 'dp', scatter_dimension=1, ti...  24.4 us
  transfers between devices with their start and end apart: 4, of which 2 were waited for; matrix products, arithmetic and copies ran while one was open for 2% of the time, Pallas kernels for 0%

commit v1 on v0

--- a/solution.py
+++ b/solution.py
@@ -109,7 +109,12 @@
         second_fix,
         routing_mask,
     )
-    routing_served = lax.all_gather(routing_out[3], ("dp", "tensor"), axis=1, tiled=True)
+    routing_served = jnp.concatenate(
+        lax.all_to_all(
+            jnp.stack([routing_out[3]] * lax.axis_size(("dp", "tensor"))), ("dp", "tensor"), 0, 0
+        ),
+        axis=1,
+    )
     return (
         attention_out[0],
         attention_out[1],

time: 544 us -> 473 us (0.87)
  blocking collectives: 222 us -> 132 us
  waiting for transfers between devices: 281 us -> 290 us
  starting transfers between devices: 0.17 us -> 8.75 us
    all_gather x1 -> x0, blocking collectives: 93.8 us -> none  [local(): lax.all_gather(routing_out[3], ('dp', 'tensor'), axis=1, tiled=True)]
    all_gather x1, waiting for transfers between devices: 0.01 us -> 9.16 us  [local(): expert_served = lax.all_gather(expert_out[3], 'dp', axis=1, tiled=True)]
    all_to_all x0 -> x1, starting transfers between devices: none -> 8.58 us  [local(): lax.all_to_all(jnp.stack([routing_out[3]] * lax.axis_size(('dp', 'tensor'...]
  transfers between devices with their start and end apart: 4 -> 5, of which waited for: 2 -> 3; matrix products, arithmetic and copies ran while one was open for 2% -> 2% of each run, Pallas kernels for 0% -> 0%
where the time goes in v1:
time: 473 us; the launch traced here: 472 us
  waiting for transfers between devices  290 us (61%)
  blocking collectives  132 us (28%)
  between operations  21.2 us (4%)
  other arithmetic  13.5 us (3%)
  starting transfers between devices  8.75 us (2%)
  local copies, waits for them, and re-layouts  6.45 us (1%)
    unnamed x5, waiting for transfers between devices  257 us
    psum x1, blocking collectives, local(): lax.psum((jnp.sum(attention_sum * attention_sum), expert_squares, jnp.sum...  79.7 us
    all_gather x1, blocking collectives, local(): lax.all_gather(attention_out[3], 'dp', axis=0, tiled=True)  52.6 us
    reduce_scatter x1, waiting for transfers between devices, local(): lax.psum_scatter(micro_total(expert_local), 'dp', scatter_dimension=1, ti...  24.4 us
  transfers between devices with their start and end apart: 5, of which 3 were waited for; matrix products, arithmetic and copies ran while one was open for 2% of the time, Pallas kernels for 0%

profile of v1, /device:TPU:1, one launch (start us, length us, event | category | flops | bytes accessed | tf_op | source)
XLA Modules:
  0.0 472.4 jit_solution(2244249464418491618)
XLA Ops:
  8.0 0.0 copy-start
  8.0 0.0 all-reduce.3.cloned.1.call-start
  8.1 1.1 copy.31
  9.1 0.7 bitcast_convert_fusion.2
  9.9 0.0 all-reduce.3.cloned.1.call-update
  9.9 0.0 reduce-scatter.3.cloned.1.call-start
  9.9 2.1 bitcast_convert_fusion.1
  12.1 0.0 reduce-scatter.3.cloned.1.call-update
  12.1 0.0 reduce-scatter.5.cloned.1.call-start
  12.2 0.0 copy-done
  12.2 2.4 bitcast_convert_fusion
  14.6 0.0 copy-start.1
  14.6 0.0 copy-start.2
  14.6 0.0 copy-start.3
  14.6 0.0 copy-start.7
  14.6 0.0 copy-start.8
  14.6 0.0 copy-start.9
  14.6 0.0 copy-start.4
  14.6 0.0 copy-start.5
  14.6 0.0 copy-start.6
  14.6 0.0 reduce-scatter.5.cloned.1.call-update
  14.7 0.0 all-gather.2.cloned.1.call-start
  16.8 256.6 %all-reduce.3.cloned.1.call-done = f32[36,512]{0,1:T(8,128)} async-done(((f32[36,512]{0,1:T(8,128)}), f32[36,512]{0,1:T(8,128)}) %all-reduce.3.cloned.1.call-update) | async-done | bytes 73744
  273.4 1.3 multiply_reduce_fusion.1
  274.7 0.0 reduce-scatter.3.cloned.1.call-done
  274.7 1.3 multiply_reduce_fusion
  276.0 24.4 %reduce-scatter.5.cloned.1.call-done = f32[2,8,1024]{2,1,0:T(8,128)} async-done(((f32[2,512,1024]{2,1,0:T(8,128)}), f32[2,8,1024]{2,1,0:T(8,128)}) %reduce-scatter.5.cloned.1.call-update) | async-done | bytes 65552 | tf_op jit(solution)/shard_map/reduce_scatter | solution.py:52
  300.5 1.4 fusion.1
  304.5 79.7 %psum.25 = f32[]{:T(128)} all-reduce(f32[]{:T(128)S(6)} %add.71), channel_id=1, replica_groups=mesh['dp'=64,'tensor'=4] {'dp','tensor'}, use_global_device_ids=true, to_apply=%region_2.0 | all-reduce | flops 1 | bytes 8 | tf_op jit(solution)/shard_map/psum | solution.py:59
  384.8 0.0 copy-done.1
  384.9 0.0 copy-done.2
  384.9 0.0 copy-done.3
  384.9 1.5 fusion.7
  386.4 0.0 all-gather.2.cloned.1.call-update
  386.5 0.0 copy-done.7
  386.5 0.0 copy-done.8
  386.5 0.0 copy-done.9
  386.5 1.3 fusion.5
  387.8 0.7 stack.2
  388.5 8.6 %all-to-all-start = ((bf16[256,36,2]{1,2,0:T(2,128)(2,1)}), bf16[256,36,2]{1,2,0:T(2,128)(2,1)S(1)}, u32[]{:S(2)}, u32[]{:S(2)}) async-start(bf16[256,36,2]{1,2,0:T(2,128)(2,1)} %stack.2), calls=%async_computation.2 | async-start | bytes 262144 | tf_op jit(solution)/shard_map/all_to_all | solution.py:113
  397.1 0.0 copy-done.4
  397.1 0.0 copy-done.5
  397.1 0.0 copy-done.6
  397.1 1.4 fusion.9
  398.5 52.6 %all_gather.6 = bf16[512,512]{1,0:T(8,128)(2,1)S(1)} all-gather(bf16[8,512]{1,0:T(8,128)(2,1)S(1)} %get-tuple-element.46), channel_id=1, replica_groups=mesh['dp'=64,'tensor'=4] {'dp'}, dimensions={0}, use_global_device_ids=true | all-gather | bytes 532480 | tf_op jit(solution)/shard_map/all_gather | solution.py:84
  451.1 0.0 all-to-all-done
  451.1 0.7 copy.32
  451.8 9.2 %all-gather.2.cloned.1.call-done = bf16[2,512,1024]{2,1,0:T(8,128)(2,1)} async-done(((bf16[2,8,1024]{2,1,0:T(8,128)(2,1)}), bf16[2,512,1024]{2,1,0:T(8,128)(2,1)}) %all-gather.2.cloned.1.call-update) | async-done | bytes 2097168 | tf_op jit(solution)/shard_map/all_gather | solution.py:98
  461.0 0.8 copy.39
  461.8 3.1 copy.40
  (1 shorter events, 0.0 us)
Async XLA Ops:
  8.0 4.1 copy-start
  8.0 265.4 %all-reduce.3.cloned.1.call-start = ((), (), s32[]{:S(2)}) async-start(), calls=%async_computation.6 | async-start | bytes 524288
  9.9 264.8 %reduce-scatter.3.cloned.1.call-start = ((), (), s32[]{:S(2)}) async-start(), calls=%async_computation.3 | async-start | bytes 1064960 | tf_op jit(solution)/shard_map/reduce_scatter | solution.py:49
  12.1 288.4 %reduce-scatter.5.cloned.1.call-start = ((), (), s32[]{:S(2)}) async-start(), calls=%async_computation.4 | async-start | bytes 4259840 | tf_op jit(solution)/shard_map/reduce_scatter | solution.py:52
  14.6 370.3 %copy-start.1 = (f32[2,8,1024]{2,1,0:T(8,128)S(1)}, f32[2,8,1024]{2,1,0:T(8,128)}, u32[]{:S(2)}) copy-start(f32[2,8,1024]{2,1,0:T(8,128)} %param.21) | copy-start | bytes 196612
  14.6 370.3 %copy-start.2 = (f32[2,8,1024]{2,1,0:T(8,128)S(1)}, f32[2,8,1024]{2,1,0:T(8,128)}, u32[]{:S(2)}) copy-start(f32[2,8,1024]{2,1,0:T(8,128)} %param.23) | copy-start | bytes 196612
  14.6 370.3 %copy-start.3 = (f32[2,8,1024]{2,1,0:T(8,128)S(1)}, f32[2,8,1024]{2,1,0:T(8,128)}, u32[]{:S(2)}) copy-start(f32[2,8,1024]{2,1,0:T(8,128)} %param.22) | copy-start | bytes 196612
  14.6 371.9 %copy-start.7 = (f32[36,2]{0,1:T(2,128)S(1)}, f32[36,2]{0,1:T(2,128)}, u32[]{:S(2)}) copy-start(f32[36,2]{0,1:T(2,128)} %param.24) | copy-start | bytes 868
  14.6 371.9 %copy-start.8 = (f32[36,2]{0,1:T(2,128)S(1)}, f32[36,2]{0,1:T(2,128)}, u32[]{:S(2)}) copy-start(f32[36,2]{0,1:T(2,128)} %param.26) | copy-start | bytes 868
  14.6 371.9 %copy-start.9 = (f32[36,2]{0,1:T(2,128)S(1)}, f32[36,2]{0,1:T(2,128)}, u32[]{:S(2)}) copy-start(f32[36,2]{0,1:T(2,128)} %param.25) | copy-start | bytes 868
  14.6 382.5 %copy-start.4 = (f32[8,512]{1,0:T(8,128)S(1)}, f32[8,512]{1,0:T(8,128)}, u32[]{:S(2)}) copy-start(f32[8,512]{1,0:T(8,128)} %param.18) | copy-start | bytes 49156
  14.6 382.5 %copy-start.5 = (f32[8,512]{1,0:T(8,128)S(1)}, f32[8,512]{1,0:T(8,128)}, u32[]{:S(2)}) copy-start(f32[8,512]{1,0:T(8,128)} %param.20) | copy-start | bytes 49156
  14.6 382.5 %copy-start.6 = (f32[8,512]{1,0:T(8,128)S(1)}, f32[8,512]{1,0:T(8,128)}, u32[]{:S(2)}) copy-start(f32[8,512]{1,0:T(8,128)} %param.19) | copy-start | bytes 49156
  14.7 446.3 %all-gather.2.cloned.1.call-start = ((), (), s32[]{:S(2)}) async-start(), calls=%async_computation.5 | async-start | bytes 2129920 | tf_op jit(solution)/shard_map/all_gather | solution.py:98
  388.5 62.6 %all-to-all-start = ((bf16[256,36,2]{1,2,0:T(2,128)(2,1)}), bf16[256,36,2]{1,2,0:T(2,128)(2,1)S(1)}, u32[]{:S(2)}, u32[]{:S(2)}) async-start(bf16[256,36,2]{1,2,0:T(2,128)(2,1)} %stack.2), calls=%async_computation.2 | async-start | bytes 262144 | tf_op jit(solution)/shard_map/all_to_all | solution.py:113
Sparse Core Ops, SparseCore 0:
  14.9 258.5 all-reduce.2
Sparse Core Ops, SparseCore 1:
  14.9 139.2 reduce-scatter.2
  158.2 142.3 reduce-scatter.4
  386.5 74.4 all-gather.1
